TPU v7x, 128 devices: a whole 4x4x4 slice. The times are simulated.
128 devices in a mesh: tok: 8 (over z, y_hi), head: 16 (over x, y_lo, core).
Axes of the slice: x: 4, y: 4 (y_hi: 2, y_lo: 2; y = y_hi * 2 + y_lo), z: 4, core: 2. Of those that a mesh axis runs over, the one named last changes fastest.
Arguments:
- states: bfloat16 [4096, 4096], P('tok', 'head'), may hold values from -400 to 400
- pre_gain: float32 [4096], replicated, may hold values from 0.5 to 1.5
- pre_shift: float32 [4096], replicated, may hold values from -1.75 to 1.75
- mlp_gain: float32 [4096], replicated, may hold values from 0.5 to 1.5
- mlp_shift: float32 [4096], replicated, may hold values from -1.75 to 1.75
- qkv_weight: bfloat16 [4096, 12288], P('tok', 'head'), may hold values from -0.09375 to 0.09375
- qkv_bias: float32 [12288], P('head'), may hold values from -1.75 to 1.75
- out_weight: bfloat16 [4096, 4096], P('head', 'tok'), may hold values from -0.125 to 0.125
- out_bias: float32 [4096], P('head'), may hold values from -1.75 to 1.75
- up_weight: bfloat16 [4096, 16384], P(None, 'head'), may hold values from -0.09375 to 0.09375
- up_bias: float32 [16384], P('head'), may hold values from -1.75 to 1.75
- down_weight: bfloat16 [16384, 4096], P('head'), may hold values from -0.0625 to 0.0625
- down_bias: float32 [4096], P('head'), may hold values from -1.75 to 1.75
- kv_cache: bfloat16 [1152, 2, 16, 4096], P(('tok', 'head')), may hold values from -320 to 320, as said below
- token_request: int32 [4096], P('tok'), may hold values from 0 to 15, as said below
- cached_len: int32 [16], P('tok'), may hold values from 128 to 1024, as said below
- page_table: int32 [16, 64], P('tok'), may hold values from 0 to 143, as said below
- migrations: int32 [64, 2], P('tok'), may hold values from 0 to 143, as said below
Outputs:
- update: bfloat16 [4096, 4096], P('tok', 'head')
Inputs may be any that keep to these rules, and one draw needn't show every extreme that they name: `token_request`: ids never fall; the tokens of request r lie among tokens (r // 2) * 512 to that plus 512 - 1, and every request has one token or more. `cached_len`: some request holds exactly 1024. `page_table`: the entries of one block are distinct. `migrations`: targets of one block are distinct and none is also a source of that block. `kv_cache`: keys are stored already rotated.
All inputs are finite; a program needn't handle non-finite values.
Results may differ from a plain program's by a relative error of at most 0.018.
The roundings to bfloat16 on the way count: a program that leaves them out, or rounds other values in their place, can miss the bound.
Values may be sent and summed in bfloat16 or wider, within the bound.
No kernel may reach another device: no remote copies, remote signals or barrier semaphores. Data moves between devices by JAX's collectives and lax.ppermute only.
A program may use at most 128 MiB of HBM per device.

v0:
```python
import jax
import jax.numpy as jnp
from jax import lax
from jax.sharding import PartitionSpec as P

HD = 128
ROT = 32
epsilon = 1e-05


def layer_norm(wide, gain, shift):
    row_mean = jnp.mean(wide, axis=1, keepdims=True)
    centred = wide - row_mean
    row_var = jnp.mean(centred * centred, axis=1, keepdims=True)
    return (centred * lax.rsqrt(row_var + epsilon) * gain + shift).astype(jnp.bfloat16)


def rotate(vectors, positions):
    half_rot = ROT // 2
    inv_freq = 10000.0 ** (-2.0 * jnp.arange(half_rot, dtype=jnp.float32) / ROT)
    angles = positions.astype(jnp.float32)[:, None] * inv_freq[None, :]
    cosine = jnp.cos(angles)[:, None, :]
    sine_part = jnp.sin(angles)[:, None, :]
    lower_half = vectors[..., :half_rot]
    upper_half = vectors[..., half_rot:ROT]
    return jnp.concatenate(
        [
            lower_half * cosine - upper_half * sine_part,
            upper_half * cosine + lower_half * sine_part,
            vectors[..., ROT:],
        ],
        axis=-1,
    )


def token_positions(local_req, cached):
    onehot = local_req[:, None] == jnp.arange(cached.shape[0], dtype=jnp.int32)[None, :]
    stretch_sizes = jnp.sum(onehot.astype(jnp.int32), axis=0)
    starts = jnp.cumsum(stretch_sizes) - stretch_sizes
    own_start = jnp.sum(jnp.where(onehot, starts[None, :], 0), axis=1)
    own_cached = jnp.sum(jnp.where(onehot, cached[None, :], 0), axis=1)
    return own_cached + jnp.arange(local_req.shape[0], dtype=jnp.int32) - own_start


def attend(queries, new_keys, new_values, cache_keys, cache_values, local_req, cached, positions):
    span = cache_keys.shape[0] // cached.shape[0]
    key_slot = jnp.arange(cache_keys.shape[0], dtype=jnp.int32)
    key_owner = key_slot // span
    key_place = key_slot % span
    cache_ok = (local_req[:, None] == key_owner[None, :]) & (
        key_place[None, :] < jnp.repeat(cached, span)[None, :]
    )
    new_ok = (local_req[:, None] == local_req[None, :]) & (positions[None, :] <= positions[:, None])
    allowed = jnp.concatenate([cache_ok, new_ok], axis=1)
    all_keys = jnp.concatenate([cache_keys, new_keys], axis=0)
    all_values = jnp.concatenate([cache_values, new_values], axis=0)
    scores = jnp.einsum(
        "thd,khd->htk", queries, all_keys, preferred_element_type=jnp.float32
    ) * HD ** (-0.5)
    scores = jnp.where(allowed[None], scores, -1e30)
    peak = jnp.max(scores, axis=2, keepdims=True)
    exp_scores = jnp.exp(scores - peak)
    attn_probs = (exp_scores / jnp.sum(exp_scores, axis=2, keepdims=True)).astype(jnp.bfloat16)
    return jnp.einsum(
        "htk,khd->thd", attn_probs, all_values, preferred_element_type=jnp.float32
    ).astype(jnp.bfloat16)


def share_pages(local_pool, groups):
    grouped = local_pool.reshape(
        local_pool.shape[0], 2, local_pool.shape[2], groups, local_pool.shape[3] // groups
    )
    shared = lax.all_to_all(grouped, "head", split_axis=3, concat_axis=0, tiled=True)
    return shared.reshape(shared.shape[0], 2, shared.shape[2], shared.shape[4])


def gather_by_all_to_all(block, axis):
    copies = jnp.concatenate([block] * lax.axis_size(axis), axis=0)
    return lax.all_to_all(copies, axis, split_axis=0, concat_axis=0, tiled=True)


def shards(
    states,
    pre_gain,
    pre_shift,
    mlp_gain,
    mlp_shift,
    qkv_weight,
    qkv_bias,
    out_weight,
    out_bias,
    up_weight,
    up_bias,
    down_weight,
    down_bias,
    kv_cache,
    token_request,
    cached_len,
    page_table,
    migrations,
):
    gathered = lax.all_gather(states, "head", axis=1, tiled=True)
    qkv_full = gather_by_all_to_all(qkv_weight, "tok")
    out_full = lax.all_gather(out_weight, "tok", axis=1, tiled=True)
    wide = gathered.astype(jnp.float32)
    pre_normed = layer_norm(wide, pre_gain, pre_shift)
    mlp_normed = layer_norm(wide, mlp_gain, mlp_shift)
    tok_rows = gathered.shape[0]
    half = tok_rows // 2

    def feed(normed):
        hidden = jax.nn.gelu(
            jnp.dot(normed, up_weight, preferred_element_type=jnp.float32) + up_bias,
            approximate=False,
        ).astype(jnp.bfloat16)
        return jnp.dot(hidden, down_weight, preferred_element_type=jnp.float32)

    feed_first = feed(mlp_normed[:half])
    kv_cache, feed_first = lax.optimization_barrier((kv_cache, feed_first))
    page_pool = share_pages(kv_cache, lax.axis_size("head"))
    joined = jnp.dot(pre_normed, qkv_full, preferred_element_type=jnp.float32)
    joined = (joined + qkv_bias).reshape(tok_rows, -1, 3, HD)
    local_req = token_request - lax.axis_index("tok") * cached_len.shape[0]
    positions = token_positions(local_req, cached_len)
    queries = rotate(joined[:, :, 0], positions).astype(jnp.bfloat16)
    new_keys = rotate(joined[:, :, 1], positions).astype(jnp.bfloat16)
    new_values = joined[:, :, 2].astype(jnp.bfloat16)
    sources = migrations[:, 0]
    targets = migrations[:, 1]
    table = page_table.reshape(-1)
    match = table[:, None] == targets[None, :]
    moved_from = jnp.sum(jnp.where(match, sources[None, :], 0), axis=1)
    table = jnp.where(jnp.any(match, axis=1), moved_from, table)
    pages = page_pool[table]
    cache_keys = pages[:, 0].reshape(-1, queries.shape[1], HD)
    cache_values = pages[:, 1].reshape(-1, queries.shape[1], HD)
    heads_out = attend(
        queries, new_keys, new_values, cache_keys, cache_values, local_req, cached_len, positions
    ).reshape(tok_rows, -1)
    attention_part = jnp.dot(heads_out, out_full, preferred_element_type=jnp.float32)
    both_first = (attention_part[:half] + feed_first).astype(jnp.bfloat16)
    both_first, normed_second = lax.optimization_barrier((both_first, mlp_normed[half:]))
    summed_first = lax.psum_scatter(both_first, "head", scatter_dimension=1, tiled=True)
    both_second = (attention_part[half:] + feed(normed_second)).astype(jnp.bfloat16)
    summed_second = lax.psum_scatter(both_second, "head", scatter_dimension=1, tiled=True)
    summed = jnp.concatenate([summed_first, summed_second], axis=0).astype(jnp.float32)
    return (summed + out_bias + down_bias).astype(jnp.bfloat16)


def solution(mesh):
    in_specs = (
        P("tok", "head"),
        P(),
        P(),
        P(),
        P(),
        P("tok", "head"),
        P("head"),
        P("head", "tok"),
        P("head"),
        P(None, "head"),
        P("head"),
        P("head", None),
        P("head"),
        P(("tok", "head"), None, None, None),
        P("tok"),
        P("tok"),
        P("tok", None),
        P("tok", None),
    )
    out_specs = P("tok", "head")
    return jax.shard_map(shards, mesh=mesh, in_specs=in_specs, out_specs=out_specs, check_vma=False)
```

profile of v0, /device:TPU:0, one launch (start us, length us, event | category | flops | bytes accessed | tf_op | source)
XLA Modules:
  0.0 333.2 jit_solution(9796448847202854535)
XLA Ops:
  12.3 2.6 copy-done.3
  14.9 8.2 %all-to-all-start.1 = ((bf16[8,512,768]{2,1,0:T(8,128)(2,1)}), bf16[8,512,768]{2,1,0:T(8,128)(2,1)}, u32[]{:S(2)}, u32[]{:S(2)}) async-start(bf16[8,512,768]{2,1,0:T(8,128)(2,1)} %bitcast.55), calls=%async_computation.1 | async-start | bytes 12582912 | tf_op jit(solution)/shard_map/all_to_all | solution.py:79
  28.8 35.1 %all-gather.3.cloned.1.call-done = bf16[512,4096]{1,0:T(8,128)(2,1)} async-done(((bf16[512,256]{1,0:T(8,128)(2,1)}), bf16[512,4096]{1,0:T(8,128)(2,1)}) %all-gather.3.cloned.1.call-update) | async-done | bytes 4194320 | tf_op jit(solution)/shard_map/all_gather | solution.py:102
  63.9 3.0 convert_reduce_fusion
  68.6 3.6 %fusion.6 = bf16[512,4096]{1,0:T(8,128)(2,1)} fusion(bf16[512,4096]{1,0:T(8,128)(2,1)S(1)} %copy-done.1, f32[4096]{0:T(1024)S(1)} %copy-done.8, f32[4096]{0:T(1024)S(1)} %copy-done.9, f32[512]{0:T(512)S(1)} %add_rsqrt_fusion, f32[512]{0:T(512)S(1)} %broadcast_multiply_fusion), kind=kLoop, calls=%fused_computation.12 | loop fusion | flops 12582912 | bytes 8425472 | tf_op jit(solution)/shard_map/convert_element_type | solution.py:15
  72.2 15.4 %fusion.68 = f32[256,4096]{1,0:T(8,128)} fusion(bf16[1024,4096]{1,0:T(8,128)(2,1)} %param.29, bf16[4096,1024]{1,0:T(8,128)(2,1)} %param.27, bf16[512,4096]{1,0:T(8,128)(2,1)} %fusion.6, f32[1024]{0:T(1024)S(1)} %copy-done.18), kind=kOutput, calls=%fused_computation.89 | convolution fusion | flops 4312268800 | bytes 23072768 | tf_op jit(solution)/shard_map/dot_general | solution.py:116
  87.6 1.8 copy.68
  89.4 27.1 %all-to-all-done.1 = bf16[8,512,768]{2,1,0:T(8,128)(2,1)} async-done(((bf16[8,512,768]{2,1,0:T(8,128)(2,1)}), bf16[8,512,768]{2,1,0:T(8,128)(2,1)}, u32[]{:S(2)}, u32[]{:S(2)}) %all-to-all-start.1) | async-done | bytes 6291488 | tf_op jit(solution)/shard_map/all_to_all | solution.py:79
  116.5 4.1 %all-to-all-start = ((bf16[9,2,16,16,256]{4,2,1,0,3:T(8,128)(2,1)}), bf16[9,2,16,16,256]{4,2,1,0,3:T(8,128)(2,1)S(1)}, u32[]{:S(2)}, u32[]{:S(2)}) async-start(bf16[9,2,16,16,256]{4,2,1,0,3:T(8,128)(2,1)} %bitcast.53), calls=%async_computation | async-start | bytes 4718592 | tf_op jit(solution)/shard_map/all_to_all | solution.py:73
  120.9 9.1 %fusion.25 = f32[512,768]{1,0:T(8,128)} fusion(bf16[4096,768]{1,0:T(8,128)(2,1)} %bitcast.9, bf16[512,4096]{1,0:T(8,128)(2,1)} %all-gather.3.cloned.1.call-done, f32[4096]{0:T(1024)S(1)} %copy-done.15, f32[4096]{0:T(1024)S(1)} %copy-done.16, f32[512]{0:T(512)S(1)} %add_rsqrt_fusion, f32[512]{0:T(512)S(1)} %broadcast_multiply_fusion, f32[768]{0:T(1024)S(1)} %copy-done.17), kind=kOutput, calls=%fused_computation.37 | convolution fusion | flops 3234201600 | bytes 12098560 | tf_op jit(solution)/shard_map/dot_general | solution.py:121
  130.0 3.1 copy.50
  133.1 2.1 fusion.217
  138.3 1.8 fusion.136
  140.1 2.5 subtract_convert_fusion.1
  142.5 8.7 %all-to-all-done = bf16[9,2,16,16,256]{4,2,1,0,3:T(8,128)(2,1)S(1)} async-done(((bf16[9,2,16,16,256]{4,2,1,0,3:T(8,128)(2,1)}), bf16[9,2,16,16,256]{4,2,1,0,3:T(8,128)(2,1)S(1)}, u32[]{:S(2)}, u32[]{:S(2)}) %all-to-all-start) | async-done | bytes 2359328 | tf_op jit(solution)/shard_map/all_to_all | solution.py:73
  151.2 2.0 gather_fusion
  157.5 10.2 %fusion.218 = (f32[2,512]{1,0:T(2,128)S(1)}, f32[2,512,2560]{2,1,0:T(8,128)}) fusion(pred[512,2560]{1,0:T(8,128)(4,1)S(1)} %copy-done.6, bf16[512,2,96]{2,0,1:T(8,128)(2,1)} %slice.112, bf16[512,2,16]{2,0,1:T(8,128)(2,1)} %get-tuple-element.25, bf16[512,2,16]{2,0,1:T(8,128)(2,1)} %get-tuple-element.26, bf16[2048,2,128]{2,0,1:T(8,128)(2,1)} %copy.57, ...), kind=kOutput, calls=%fused_computation.272 | convolution fusion | flops 687606272 | bytes 13373440 | tf_op jit(solution)/shard_map/sub | solution.py:62
  167.7 5.9 %fusion.42 = bf16[2,128,512]{2,1,0:T(8,128)(2,1)S(1)} fusion(f32[2,512,2560]{2,1,0:T(8,128)} %get-tuple-element.32, f32[2,512]{1,0:T(2,128)S(1)} %get-tuple-element.31, bf16[512,2,128]{0,2,1:T(8,128)(2,1)S(1)} %copy-done.7, bf16[2048,2,128]{0,2,1:T(8,128)(2,1)S(1)} %copy.52), kind=kOutput, calls=%fused_computation.51 | convolution fusion | flops 679084032 | bytes 12062720 | tf_op jit(solution)/shard_map/htk,khd->thd/dot_general | solution.py:64
  173.6 3.0 fusion.221
  176.6 3.2 copy-done.2
  179.9 1.9 fusion.18
  181.7 15.1 %fusion.15 = bf16[256,4096]{1,0:T(8,128)(2,1)} fusion(bf16[1024,4096]{1,0:T(8,128)(2,1)} %param.29, f32[512,4096]{1,0:T(8,128)} %copy-done.2, bf16[256,4096]{1,0:T(8,128)(2,1)S(1)} %slice-done, bf16[4096,1024]{1,0:T(8,128)(2,1)} %param.27, f32[1024]{0:T(1024)S(1)} %copy-done.18), kind=kOutput, calls=%fused_computation.23 | convolution fusion | flops 4314365952 | bytes 25169920 | tf_op jit(solution)/shard_map/dot_general | solution.py:116
  197.4 62.5 %reduce-scatter.5.cloned.1.call-done = bf16[256,256]{1,0:T(8,128)(2,1)} async-done(((bf16[256,4096]{1,0:T(8,128)(2,1)}), bf16[256,256]{1,0:T(8,128)(2,1)}) %reduce-scatter.5.cloned.1.call-update) | async-done | bytes 131088 | tf_op jit(solution)/shard_map/reduce_scatter | solution.py:145
  260.0 64.9 %reduce-scatter.3.cloned.1.call-done = bf16[256,256]{1,0:T(8,128)(2,1)} async-done(((bf16[256,4096]{1,0:T(8,128)(2,1)}), bf16[256,256]{1,0:T(8,128)(2,1)}) %reduce-scatter.3.cloned.1.call-update) | async-done | bytes 131088 | tf_op jit(solution)/shard_map/reduce_scatter | solution.py:143
  (93 shorter events, 23.0 us)
Async XLA Ops:
  6.5 5.5 %copy-start = (bf16[512,768]{1,0:T(8,128)(2,1)S(1)}, bf16[512,768]{1,0:T(8,128)(2,1)}, u32[]{:S(2)}) copy-start(bf16[512,768]{1,0:T(8,128)(2,1)} %param.23) | copy-start | bytes 2359300
  6.5 57.4 %all-gather.3.cloned.1.call-start = ((), (), s32[]{:S(2)}) async-start(), calls=%async_computation.4 | async-start | bytes 4456448 | tf_op jit(solution)/shard_map/all_gather | solution.py:102
  14.9 9.0 %copy-start.19 = (s32[2,64]{1,0:T(2,128)S(1)}, s32[2,64]{1,0:T(2,128)}, u32[]{:S(2)}) copy-start(s32[2,64]{1,0:T(2,128)} %param.34) | copy-start | bytes 1540
  14.9 9.1 %copy-start.11 = (s32[512]{0:T(512)S(1)}, s32[512]{0:T(512)}, u32[]{:S(2)}) copy-start(s32[512]{0:T(512)} %param.32) | copy-start | bytes 6148
  14.9 9.4 %copy-start.10 = (s32[2]{0:T(128)S(1)}, s32[2]{0:T(128)}, u32[]{:S(2)}) copy-start(s32[2]{0:T(128)} %param.33) | copy-start | bytes 28
  14.9 11.5 %copy-start.14 = (s32[8,2]{0,1:T(2,128)S(1)}, s32[8,2]{0,1:T(2,128)}, u32[]{:S(2)}) copy-start(s32[8,2]{0,1:T(2,128)} %param.35) | copy-start | bytes 196
  14.9 101.6 %all-to-all-start.1 = ((bf16[8,512,768]{2,1,0:T(8,128)(2,1)}), bf16[8,512,768]{2,1,0:T(8,128)(2,1)}, u32[]{:S(2)}, u32[]{:S(2)}) async-start(bf16[8,512,768]{2,1,0:T(8,128)(2,1)} %bitcast.55), calls=%async_computation.1 | async-start | bytes 12582912 | tf_op jit(solution)/shard_map/all_to_all | solution.py:79
  23.1 150.5 %all-gather.5.cloned.1.call-start = ((), (), s32[]{:S(2)}) async-start(), calls=%async_computation.5 | async-start | bytes 2359296 | tf_op jit(solution)/shard_map/all_gather | solution.py:104
  25.6 43.0 %copy-start.8 = (f32[4096]{0:T(1024)S(1)}, f32[4096]{0:T(1024)}, u32[]{:S(2)}) copy-start(f32[4096]{0:T(1024)} %param.22) | copy-start | bytes 49156
  25.6 43.0 %copy-start.9 = (f32[4096]{0:T(1024)S(1)}, f32[4096]{0:T(1024)}, u32[]{:S(2)}) copy-start(f32[4096]{0:T(1024)} %param.21) | copy-start | bytes 49156
  63.9 3.4 %copy-start.1 = (bf16[512,4096]{1,0:T(8,128)(2,1)S(1)}, bf16[512,4096]{1,0:T(8,128)(2,1)}, u32[]{:S(2)}) copy-start(bf16[512,4096]{1,0:T(8,128)(2,1)} %all-gather.3.cloned.1.call-done) | copy-start | bytes 12582916
  67.4 4.8 %copy-start.18 = (f32[1024]{0:T(1024)S(1)}, f32[1024]{0:T(1024)}, u32[]{:S(2)}) copy-start(f32[1024]{0:T(1024)} %param.28) | copy-start | bytes 12292
  72.2 15.4 %copy-start.5 = (bf16[9,2,16,4096]{3,2,1,0:T(8,128)(2,1)S(1)}, bf16[9,2,16,4096]{3,2,1,0:T(8,128)(2,1)}, u32[]{:S(2)}) copy-start(bf16[9,2,16,4096]{3,2,1,0:T(8,128)(2,1)} %param.31) | copy-start | bytes 7077892
  87.6 33.3 %copy-start.15 = (f32[4096]{0:T(1024)S(1)}, f32[4096]{0:T(1024)}, u32[]{:S(2)}) copy-start(f32[4096]{0:T(1024)} %param.20) | copy-start | bytes 49156
  87.6 33.3 %copy-start.16 = (f32[4096]{0:T(1024)S(1)}, f32[4096]{0:T(1024)}, u32[]{:S(2)}) copy-start(f32[4096]{0:T(1024)} %param.19) | copy-start | bytes 49156
  87.6 33.3 %copy-start.17 = (f32[768]{0:T(1024)S(1)}, f32[768]{0:T(1024)}, u32[]{:S(2)}) copy-start(f32[768]{0:T(1024)} %param.24) | copy-start | bytes 9220
  116.5 34.7 %all-to-all-start = ((bf16[9,2,16,16,256]{4,2,1,0,3:T(8,128)(2,1)}), bf16[9,2,16,16,256]{4,2,1,0,3:T(8,128)(2,1)S(1)}, u32[]{:S(2)}, u32[]{:S(2)}) async-start(bf16[9,2,16,16,256]{4,2,1,0,3:T(8,128)(2,1)} %bitcast.53), calls=%async_computation | async-start | bytes 4718592 | tf_op jit(solution)/shard_map/all_to_all | solution.py:73
  120.6 139.4 %reduce-scatter.5.cloned.1.call-start = ((), (), s32[]{:S(2)}) async-start(), calls=%async_computation.7 | async-start | bytes 2228224 | tf_op jit(solution)/shard_map/reduce_scatter | solution.py:145
  157.5 10.2 %copy-start.7 = (bf16[512,2,128]{0,2,1:T(8,128)(2,1)S(1)}, bf16[512,2,128]{0,2,1:T(8,128)(2,1)}, u32[]{:S(2)}) copy-start(bf16[512,2,128]{0,2,1:T(8,128)(2,1)} %fusion.136) | copy-start | bytes 786436
  173.6 6.3 %copy-start.4 = (f32[256,4096]{1,0:T(8,128)S(1)}, f32[256,4096]{1,0:T(8,128)}, u32[]{:S(2)}) copy-start(f32[256,4096]{1,0:T(8,128)} %fusion.68) | copy-start | bytes 12582916
  176.6 3.2 copy-start.2
  181.7 143.1 %copy-start.12 = (f32[256]{0:T(256)S(1)}, f32[256]{0:T(256)}, u32[]{:S(2)}) copy-start(f32[256]{0:T(256)} %param.30) | copy-start | bytes 3076
  181.7 143.1 %copy-start.13 = (f32[256]{0:T(256)S(1)}, f32[256]{0:T(256)}, u32[]{:S(2)}) copy-start(f32[256]{0:T(256)} %param.26) | copy-start | bytes 3076
  196.9 128.0 %reduce-scatter.3.cloned.1.call-start = ((), (), s32[]{:S(2)}) async-start(), calls=%async_computation.6 | async-start | bytes 2228224 | tf_op jit(solution)/shard_map/reduce_scatter | solution.py:143
  (3 other events, 6.8 us)
Sparse Core Ops, SparseCore 0:
  9.0 54.9 all-gather.2
  66.1 83.3 all-gather.4
  197.0 62.9 reduce-scatter.4
  262.2 62.6 reduce-scatter.2
where the time goes:
time: 334 us; the launch traced here: 333 us
  waiting for transfers between devices  200 us (60%)
  matrix products  58.7 us (18%)
  local copies, waits for them, and re-layouts  31.3 us (9%)
  other arithmetic  16.8 us (5%)
  between operations  13.4 us (4%)
  starting transfers between devices  12.6 us (4%)
    reduce_scatter x1, waiting for transfers between devices, shards(): lax.psum_scatter(both_first, 'head', scatter_dimension=1, tiled=True)  64.9 us
    reduce_scatter x1, waiting for transfers between devices, shards(): lax.psum_scatter(both_second, 'head', scatter_dimension=1, tiled=True)  62.5 us
    all_gather x1, waiting for transfers between devices, shards(): gathered = lax.all_gather(states, 'head', axis=1, tiled=True)  35.1 us
    dot_general x2, matrix products, feed(): return jnp.dot(hidden, down_weight, preferred_element_type=jnp.float32)  30.5 us
    all_to_all x1, waiting for transfers between devices, gather_by_all_to_all(): return lax.all_to_all(copies, axis, split_axis=0, concat_axis=0, tiled=True)  27.1 us
    unnamed x50, local copies, waits for them, and re-layouts  12.8 us
    sub x1, matrix products, attend(): exp_scores = jnp.exp(scores - peak)  10.2 us
    dot_general x1, matrix products, shards(): joined = jnp.dot(pre_normed, qkv_full, preferred_element_type=jnp.float32)  9.12 us
  transfers between devices with their start and end apart: 6, of which 5 were waited for; matrix products, arithmetic and copies ran while one was open for 24% of the time, Pallas kernels for 0%

commit v1 on v0

--- a/solution.py
+++ b/solution.py
@@ -99,7 +99,12 @@
     page_table,
     migrations,
 ):
-    gathered = lax.all_gather(states, "head", axis=1, tiled=True)
+    gathered = jnp.concatenate(
+        jax.lax.all_to_all(
+            jnp.stack([states for _ in range(jax.lax.psum(1, "head"))], axis=0), "head", 0, 0
+        ),
+        axis=1,
+    )
     qkv_full = gather_by_all_to_all(qkv_weight, "tok")
     out_full = lax.all_gather(out_weight, "tok", axis=1, tiled=True)
     wide = gathered.astype(jnp.float32)

time: 334 us -> 384 us (1.15)
  waiting for transfers between devices: 200 us -> 237 us
  starting transfers between devices: 12.6 us -> 23.8 us
  other arithmetic: 16.8 us -> 23.1 us
    all_to_all x0 -> x1, waiting for transfers between devices: none -> 47.7 us  [shards(): jax.lax.all_to_all(jnp.stack([states for _ in range(jax.lax.psum(1, 'head...]
    all_gather x1 -> x0, waiting for transfers between devices: 35.1 us -> none  [shards(): gathered = lax.all_gather(states, 'head', axis=1, tiled=True)]
    all_to_all x1, waiting for transfers between devices: 27.1 us -> 53.9 us  [gather_by_all_to_all(): return lax.all_to_all(copies, axis, split_axis=0, concat_axis=0, tiled=True)]
    all_to_all x1, starting transfers between devices: 4.08 us -> 10.2 us  [share_pages(): lax.all_to_all(grouped, 'head', split_axis=3, concat_axis=0, tiled=True)]
    all_to_all x0 -> x1, starting transfers between devices: none -> 5.69 us  [shards(): jax.lax.all_to_all(jnp.stack([states for _ in range(jax.lax.psum(1, 'head...]
    convert_element_type x1 -> x2, other arithmetic: 3.55 us -> 7.7 us  [layer_norm(): (centred * lax.rsqrt(row_var + epsilon) * gain + shift).astype(jnp.bfloat16)]
    unnamed x50 -> x49, local copies, waits for them, and re-layouts: 12.8 us -> 8.88 us
  transfers between devices with their start and end apart: 6 -> 6, of which waited for: 5 -> 5; matrix products, arithmetic and copies ran while one was open for 24% -> 20% of each run, Pallas kernels for 0% -> 0%
where the time goes in v1:
time: 384 us
  waiting for transfers between devices  237 us (62%)
  matrix products  56.4 us (15%)
  local copies, waits for them, and re-layouts  29.7 us (8%)
  starting transfers between devices  23.8 us (6%)
  other arithmetic  23.1 us (6%)
  between operations  13.5 us (4%)
    reduce_scatter x1, waiting for transfers between devices, shards(): lax.psum_scatter(both_first, 'head', scatter_dimension=1, tiled=True)  64.8 us
    reduce_scatter x1, waiting for transfers between devices, shards(): lax.psum_scatter(both_second, 'head', scatter_dimension=1, tiled=True)  61.5 us
    all_to_all x1, waiting for transfers between devices, gather_by_all_to_all(): return lax.all_to_all(copies, axis, split_axis=0, concat_axis=0, tiled=True)  53.9 us
    all_to_all x1, waiting for transfers between devices, shards(): jax.lax.all_to_all(jnp.stack([states for _ in range(jax.lax.psum(1, 'head...  47.7 us
    dot_general x2, matrix products, feed(): return jnp.dot(hidden, down_weight, preferred_element_type=jnp.float32)  30.4 us
    all_to_all x1, starting transfers between devices, share_pages(): lax.all_to_all(grouped, 'head', split_axis=3, concat_axis=0, tiled=True)  10.2 us
    sub x1, matrix products, attend(): exp_scores = jnp.exp(scores - peak)  10.2 us
    unnamed x49, local copies, waits for them, and re-layouts  8.88 us
  transfers between devices with their start and end apart: 6, of which 5 were waited for; matrix products, arithmetic and copies ran while one was open for 20% of the time, Pallas kernels for 0%

profile of v1, /device:TPU:0, one launch (start us, length us, event | category | flops | bytes accessed | tf_op | source)
XLA Modules:
  0.0 383.6 jit_solution(17580532539073541072)
XLA Ops:
  7.6 2.3 stack.2
  10.0 5.7 %all-to-all-start = ((bf16[16,512,256]{1,2,0:T(8,128)(2,1)}), bf16[16,512,256]{1,2,0:T(8,128)(2,1)}, u32[]{:S(2)}, u32[]{:S(2)}) async-start(bf16[16,512,256]{1,2,0:T(8,128)(2,1)} %stack.2), calls=%async_computation | async-start | bytes 8388608 | tf_op jit(solution)/shard_map/all_to_all | solution.py:103
  17.7 2.6 copy-done.2
  20.6 47.7 %all-to-all-done = bf16[16,512,256]{1,2,0:T(8,128)(2,1)} async-done(((bf16[16,512,256]{1,2,0:T(8,128)(2,1)}), bf16[16,512,256]{1,2,0:T(8,128)(2,1)}, u32[]{:S(2)}, u32[]{:S(2)}) %all-to-all-start) | async-done | bytes 4194336 | tf_op jit(solution)/shard_map/all_to_all | solution.py:103
  68.3 7.8 %all-to-all-start.2 = ((bf16[8,512,768]{2,1,0:T(8,128)(2,1)}), bf16[8,512,768]{2,1,0:T(8,128)(2,1)}, u32[]{:S(2)}, u32[]{:S(2)}) async-start(bf16[8,512,768]{2,1,0:T(8,128)(2,1)} %bitcast.71), calls=%async_computation.2 | async-start | bytes 12582912 | tf_op jit(solution)/shard_map/all_to_all | solution.py:79
  80.0 2.8 convert_reduce_fusion
  82.9 3.5 multiply_reduce_fusion
  86.4 4.5 %fusion.4 = bf16[512,4096]{0,1:T(8,128)(2,1)} fusion(bf16[16,512,256]{1,2,0:T(8,128)(2,1)} %all-to-all-done, f32[4096]{0:T(1024)S(1)} %copy-done.7, f32[4096]{0:T(1024)S(1)} %copy-done.8, f32[512]{0:T(512)S(1)} %add_rsqrt_fusion, f32[512]{0:T(512)S(1)} %broadcast_multiply_fusion), kind=kLoop, calls=%fused_computation.9 | loop fusion | flops 12582912 | bytes 8425472 | tf_op jit(solution)/shard_map/convert_element_type | solution.py:15
  90.9 15.3 %fusion.54 = f32[256,4096]{1,0:T(8,128)} fusion(bf16[1024,4096]{1,0:T(8,128)(2,1)} %param.29, bf16[4096,1024]{1,0:T(8,128)(2,1)} %param.27, bf16[512,4096]{0,1:T(8,128)(2,1)} %fusion.4, f32[1024]{0:T(1024)S(1)} %copy-done.17), kind=kOutput, calls=%fused_computation.81 | convolution fusion | flops 4312268800 | bytes 23072768 | tf_op jit(solution)/shard_map/dot_general | solution.py:121
  108.0 53.9 %all-to-all-done.2 = bf16[8,512,768]{2,1,0:T(8,128)(2,1)} async-done(((bf16[8,512,768]{2,1,0:T(8,128)(2,1)}), bf16[8,512,768]{2,1,0:T(8,128)(2,1)}, u32[]{:S(2)}, u32[]{:S(2)}) %all-to-all-start.2) | async-done | bytes 6291488 | tf_op jit(solution)/shard_map/all_to_all | solution.py:79
  161.8 10.2 %all-to-all-start.1 = ((bf16[9,2,16,16,256]{4,2,1,0,3:T(8,128)(2,1)}), bf16[9,2,16,16,256]{4,2,1,0,3:T(8,128)(2,1)S(1)}, u32[]{:S(2)}, u32[]{:S(2)}) async-start(bf16[9,2,16,16,256]{4,2,1,0,3:T(8,128)(2,1)} %bitcast.69), calls=%async_computation.1 | async-start | bytes 4718592 | tf_op jit(solution)/shard_map/all_to_all | solution.py:73
  172.1 3.2 add_convert_fusion
  175.4 6.9 %convolution_add_fusion.1 = f32[512,768]{1,0:T(8,128)} fusion(bf16[512,4096]{0,1:T(8,128)(2,1)S(1)} %bitcast.78, bf16[4096,768]{1,0:T(8,128)(2,1)} %bitcast.13, f32[768]{0:T(1024)S(1)} %copy-done.16), kind=kOutput, calls=%fused_computation.29 | convolution fusion | flops 3221618688 | bytes 12061696 | tf_op jit(solution)/shard_map/dot_general | solution.py:126
  182.3 3.0 copy.55
  185.3 2.1 fusion.203
  192.3 2.5 subtract_convert_fusion.1
  194.8 7.9 %all-to-all-done.1 = bf16[9,2,16,16,256]{4,2,1,0,3:T(8,128)(2,1)S(1)} async-done(((bf16[9,2,16,16,256]{4,2,1,0,3:T(8,128)(2,1)}), bf16[9,2,16,16,256]{4,2,1,0,3:T(8,128)(2,1)S(1)}, u32[]{:S(2)}, u32[]{:S(2)}) %all-to-all-start.1) | async-done | bytes 2359328 | tf_op jit(solution)/shard_map/all_to_all | solution.py:73
  208.9 10.2 %fusion.204 = (f32[2,512]{1,0:T(2,128)S(1)}, f32[2,512,2560]{2,1,0:T(8,128)}) fusion(pred[512,2560]{1,0:T(8,128)(4,1)S(1)} %copy-done.5, bf16[512,2,96]{2,0,1:T(8,128)(2,1)} %slice.112, bf16[512,2,16]{2,0,1:T(8,128)(2,1)} %get-tuple-element.25, bf16[512,2,16]{2,0,1:T(8,128)(2,1)} %get-tuple-element.26, bf16[2048,2,128]{2,0,1:T(8,128)(2,1)} %copy.62, ...), kind=kOutput, calls=%fused_computation.264 | convolution fusion | flops 687606272 | bytes 13373440 | tf_op jit(solution)/shard_map/sub | solution.py:62
  219.1 5.9 %fusion.28 = bf16[2,128,512]{2,1,0:T(8,128)(2,1)S(1)} fusion(f32[2,512,2560]{2,1,0:T(8,128)} %get-tuple-element.32, f32[2,512]{1,0:T(2,128)S(1)} %get-tuple-element.31, bf16[512,2,128]{0,2,1:T(8,128)(2,1)S(1)} %copy-done.6, bf16[2048,2,128]{0,2,1:T(8,128)(2,1)S(1)} %copy.57), kind=kOutput, calls=%fused_computation.43 | convolution fusion | flops 679084032 | bytes 12062720 | tf_op jit(solution)/shard_map/htk,khd->thd/dot_general | solution.py:64
  225.0 3.0 fusion.207
  228.1 3.2 copy-done.1
  233.2 15.1 %fusion.10 = bf16[256,4096]{1,0:T(8,128)(2,1)} fusion(bf16[1024,4096]{1,0:T(8,128)(2,1)} %param.29, f32[512,4096]{1,0:T(8,128)} %copy-done.1, bf16[256,4096]{0,1:T(8,128)(2,1)S(1)} %slice-done, bf16[4096,1024]{1,0:T(8,128)(2,1)} %param.27, f32[1024]{0:T(1024)S(1)} %copy-done.17), kind=kOutput, calls=%fused_computation.20 | convolution fusion | flops 4314365952 | bytes 25169920 | tf_op jit(solution)/shard_map/dot_general | solution.py:121
  249.0 61.5 %reduce-scatter.5.cloned.1.call-done = bf16[256,256]{1,0:T(8,128)(2,1)} async-done(((bf16[256,4096]{1,0:T(8,128)(2,1)}), bf16[256,256]{1,0:T(8,128)(2,1)}) %reduce-scatter.5.cloned.1.call-update) | async-done | bytes 131088 | tf_op jit(solution)/shard_map/reduce_scatter | solution.py:150
  310.5 64.8 %reduce-scatter.3.cloned.1.call-done = bf16[256,256]{1,0:T(8,128)(2,1)} async-done(((bf16[256,4096]{1,0:T(8,128)(2,1)}), bf16[256,256]{1,0:T(8,128)(2,1)}) %reduce-scatter.3.cloned.1.call-update) | async-done | bytes 131088 | tf_op jit(solution)/shard_map/reduce_scatter | solution.py:148
  (95 shorter events, 24.5 us)
Async XLA Ops:
  10.0 6.5 %copy-start.18 = (s32[2,64]{1,0:T(2,128)S(1)}, s32[2,64]{1,0:T(2,128)}, u32[]{:S(2)}) copy-start(s32[2,64]{1,0:T(2,128)} %param.34) | copy-start | bytes 1540
  10.0 6.6 %copy-start.12 = (s32[512]{0:T(512)S(1)}, s32[512]{0:T(512)}, u32[]{:S(2)}) copy-start(s32[512]{0:T(512)} %param.32) | copy-start | bytes 6148
  10.0 7.0 %copy-start.15 = (s32[8,2]{0,1:T(2,128)S(1)}, s32[8,2]{0,1:T(2,128)}, u32[]{:S(2)}) copy-start(s32[8,2]{0,1:T(2,128)} %param.35) | copy-start | bytes 196
  10.0 7.2 %copy-start.11 = (s32[2]{0:T(128)S(1)}, s32[2]{0:T(128)}, u32[]{:S(2)}) copy-start(s32[2]{0:T(128)} %param.33) | copy-start | bytes 28
  10.0 7.2 %copy-start = (bf16[512,768]{1,0:T(8,128)(2,1)S(1)}, bf16[512,768]{1,0:T(8,128)(2,1)}, u32[]{:S(2)}) copy-start(bf16[512,768]{1,0:T(8,128)(2,1)} %param.23) | copy-start | bytes 2359300
  10.0 58.3 %all-to-all-start = ((bf16[16,512,256]{1,2,0:T(8,128)(2,1)}), bf16[16,512,256]{1,2,0:T(8,128)(2,1)}, u32[]{:S(2)}, u32[]{:S(2)}) async-start(bf16[16,512,256]{1,2,0:T(8,128)(2,1)} %stack.2), calls=%async_computation | async-start | bytes 8388608 | tf_op jit(solution)/shard_map/all_to_all | solution.py:103
  15.7 209.3 %all-gather.2.cloned.1.call-start = ((), (), s32[]{:S(2)}) async-start(), calls=%async_computation.5 | async-start | bytes 2359296 | tf_op jit(solution)/shard_map/all_gather | solution.py:109
  17.7 2.6 copy-start.2
  68.3 9.5 %copy-start.9 = (f32[4096]{0:T(1024)S(1)}, f32[4096]{0:T(1024)}, u32[]{:S(2)}) copy-start(f32[4096]{0:T(1024)} %param.20) | copy-start | bytes 49156
  68.3 9.5 %copy-start.10 = (f32[4096]{0:T(1024)S(1)}, f32[4096]{0:T(1024)}, u32[]{:S(2)}) copy-start(f32[4096]{0:T(1024)} %param.19) | copy-start | bytes 49156
  68.3 93.5 %all-to-all-start.2 = ((bf16[8,512,768]{2,1,0:T(8,128)(2,1)}), bf16[8,512,768]{2,1,0:T(8,128)(2,1)}, u32[]{:S(2)}, u32[]{:S(2)}) async-start(bf16[8,512,768]{2,1,0:T(8,128)(2,1)} %bitcast.71), calls=%async_computation.2 | async-start | bytes 12582912 | tf_op jit(solution)/shard_map/all_to_all | solution.py:79
  78.9 7.5 %copy-start.7 = (f32[4096]{0:T(1024)S(1)}, f32[4096]{0:T(1024)}, u32[]{:S(2)}) copy-start(f32[4096]{0:T(1024)} %param.22) | copy-start | bytes 49156
  78.9 7.5 %copy-start.8 = (f32[4096]{0:T(1024)S(1)}, f32[4096]{0:T(1024)}, u32[]{:S(2)}) copy-start(f32[4096]{0:T(1024)} %param.21) | copy-start | bytes 49156
  86.3 4.5 %copy-start.17 = (f32[1024]{0:T(1024)S(1)}, f32[1024]{0:T(1024)}, u32[]{:S(2)}) copy-start(f32[1024]{0:T(1024)} %param.28) | copy-start | bytes 12292
  90.9 15.3 %copy-start.4 = (bf16[9,2,16,4096]{3,2,1,0:T(8,128)(2,1)S(1)}, bf16[9,2,16,4096]{3,2,1,0:T(8,128)(2,1)}, u32[]{:S(2)}) copy-start(bf16[9,2,16,4096]{3,2,1,0:T(8,128)(2,1)} %param.31) | copy-start | bytes 7077892
  161.8 40.8 %all-to-all-start.1 = ((bf16[9,2,16,16,256]{4,2,1,0,3:T(8,128)(2,1)}), bf16[9,2,16,16,256]{4,2,1,0,3:T(8,128)(2,1)S(1)}, u32[]{:S(2)}, u32[]{:S(2)}) async-start(bf16[9,2,16,16,256]{4,2,1,0,3:T(8,128)(2,1)} %bitcast.69), calls=%async_computation.1 | async-start | bytes 4718592 | tf_op jit(solution)/shard_map/all_to_all | solution.py:73
  172.1 3.3 copy-start.16
  172.1 138.5 %reduce-scatter.5.cloned.1.call-start = ((), (), s32[]{:S(2)}) async-start(), calls=%async_computation.7 | async-start | bytes 2228224 | tf_op jit(solution)/shard_map/reduce_scatter | solution.py:150
  208.9 10.2 %copy-start.6 = (bf16[512,2,128]{0,2,1:T(8,128)(2,1)S(1)}, bf16[512,2,128]{0,2,1:T(8,128)(2,1)}, u32[]{:S(2)}) copy-start(bf16[512,2,128]{0,2,1:T(8,128)(2,1)} %fusion.122) | copy-start | bytes 786436
  225.0 6.3 %copy-start.3 = (f32[256,4096]{1,0:T(8,128)S(1)}, f32[256,4096]{1,0:T(8,128)}, u32[]{:S(2)}) copy-start(f32[256,4096]{1,0:T(8,128)} %fusion.54) | copy-start | bytes 12582916
  228.1 3.2 copy-start.1
  233.2 142.2 %copy-start.13 = (f32[256]{0:T(256)S(1)}, f32[256]{0:T(256)}, u32[]{:S(2)}) copy-start(f32[256]{0:T(256)} %param.30) | copy-start | bytes 3076
  233.2 142.2 %copy-start.14 = (f32[256]{0:T(256)S(1)}, f32[256]{0:T(256)}, u32[]{:S(2)}) copy-start(f32[256]{0:T(256)} %param.26) | copy-start | bytes 3076
  248.3 127.0 %reduce-scatter.3.cloned.1.call-start = ((), (), s32[]{:S(2)}) async-start(), calls=%async_computation.6 | async-start | bytes 2228224 | tf_op jit(solution)/shard_map/reduce_scatter | solution.py:148
  (2 other events, 4.1 us)
Sparse Core Ops, SparseCore 0:
  18.7 131.0 all-gather.1
  248.4 62.0 reduce-scatter.4
  312.9 62.3 reduce-scatter.2
